TPU v7x, 256 devices: a whole 4x4x8 slice. The times are simulated.
256 devices in a mesh: chan: 32 (over y_hi, z, core), win: 8 (over x, y_lo).
Axes of the slice: x: 4, y: 4 (y_hi: 2, y_lo: 2; y = y_hi * 2 + y_lo), z: 8, core: 2. Of those that a mesh axis runs over, the one named last changes fastest.
Arguments:
- traces: bfloat16 [8, 1024, 8192], P('win', 'chan'), may hold values from -6 to 6
- owner: int32 [3], replicated, may hold values from 0 to 31
- window_mask: int32 [8, 32], P('win', 'chan'), may hold values 0 or 1
Outputs:
- stacks: float32 [3, 32, 64, 1024], P(None, None, 'win', 'chan')
Inputs may be any that keep to these rules, and one draw needn't show every extreme that they name: `owner`: each step names one channel block.
All inputs are finite; a program needn't handle non-finite values. No bound on the sum of `window_mask` on one device may be relied on, other than what follows from the above.
Results may differ from a plain program's by a relative error of at most 0.0028.
Values may be sent and summed in bfloat16 or wider, within the bound.
No kernel may reach another device: no remote copies, remote signals or barrier semaphores. Data moves between devices by JAX's collectives and lax.ppermute only.
A program may use at most 128 MiB of HBM per device.

v0:
```python
import math
import jax
import jax.numpy as jnp
from jax import lax
from jax.sharding import PartitionSpec as P

LAGS = 64


def spread(value, axis, source):
    kept = jnp.where(lax.axis_index(axis) == source, value, 0).astype(value.dtype)
    return lax.psum(kept, axis)


def body(traces, owner, window_mask):
    chan_dev = traces.shape[1]
    samples = traces.shape[2]
    step_count = owner.shape[0]
    signal = traces[0].astype(jnp.float32)
    whitened = (
        signal * lax.rsqrt(jnp.mean(signal * signal, axis=-1, keepdims=True) + 1e-06)
    ).astype(jnp.bfloat16)
    own_flag = window_mask[0, 0].astype(jnp.float32)
    outgoing = whitened * own_flag.astype(jnp.bfloat16)
    received = [spread(outgoing, "chan", owner[step]) for step in range(step_count)]
    sources = jnp.concatenate(received, 0)
    padded = jnp.pad(whitened, ((0, 0), (64, 64)))
    half_lags = LAGS // 2
    win_count = lax.axis_size("win")
    per_dev = LAGS // win_count
    time_block = min(samples, 4096)
    factor = own_flag / math.sqrt(samples)

    def group_lags(which):
        return list(range(which * 8, which * 8 + 8))

    def correlate(lag_values):
        summed = jnp.zeros((sources.shape[0], len(lag_values), chan_dev), jnp.float32)
        for offset in range(0, samples, time_block):
            shifted = jnp.stack(
                [
                    padded[
                        :,
                        offset + lag - half_lags + 64 : offset + lag - half_lags + 64 + time_block,
                    ]
                    for lag in lag_values
                ],
                0,
            )
            summed = summed + jnp.einsum(
                "pt,gct->pgc",
                sources[:, offset : offset + time_block],
                shifted,
                preferred_element_type=jnp.float32,
            )
        return summed * factor

    complete = jnp.concatenate([correlate(group_lags(which)) for which in range(LAGS // 8)], 1)
    reduced = lax.psum_scatter(complete, "win", scatter_dimension=1, tiled=True)
    return reduced.reshape(step_count, chan_dev, per_dev, chan_dev)


def solution(mesh):
    return jax.shard_map(
        body,
        mesh=mesh,
        in_specs=(P("win", "chan", None), P(), P("win", "chan")),
        out_specs=P(None, None, "win", "chan"),
        check_vma=False,
    )
```

profile of v0, /device:TPU:16, one launch (start us, length us, event | category | flops | bytes accessed | tf_op | source)
XLA Modules:
  0.0 365.3 jit_solution(5036008442695685828)
XLA Ops:
  7.2 1.3 fusion.16
  8.5 1.4 fusion.27
  11.8 2.1 broadcast_select_fusion
  13.9 1.1 broadcast_select_fusion.1
  15.0 0.2 constant_dynamic-update-slice_fusion.34
  15.3 0.6 constant_dynamic-update-slice_fusion.122
  15.9 0.7 constant_dynamic-update-slice_fusion.130
  16.7 0.7 constant_dynamic-update-slice_fusion.129
  17.4 0.7 constant_dynamic-update-slice_fusion.128
  18.1 0.7 constant_dynamic-update-slice_fusion.127
  18.9 0.7 constant_dynamic-update-slice_fusion.126
  19.6 0.7 constant_dynamic-update-slice_fusion.125
  20.3 1.3 copy-done.20
  21.7 0.6 constant_dynamic-update-slice_fusion.124
  22.7 1.0 copy-done.14
  23.7 2.1 constant_dynamic-update-slice_fusion.123
  25.7 0.1 constant_dynamic-update-slice_fusion.113
  25.9 0.1 constant_dynamic-update-slice_fusion.112
  26.2 0.1 constant_dynamic-update-slice_fusion.110
  26.5 0.2 constant_dynamic-update-slice_fusion.108
  27.4 1.3 constant_dynamic-update-slice_fusion.107
  28.7 1.6 constant_dynamic-update-slice_fusion.91
  30.8 1.3 constant_dynamic-update-slice_fusion.75
  32.0 1.0 constant_dynamic-update-slice_fusion.54
  33.0 0.8 constant_dynamic-update-slice_fusion.53
  33.9 0.8 constant_dynamic-update-slice_fusion.52
  34.7 1.2 constant_dynamic-update-slice_fusion.51
  35.9 0.9 constant_dynamic-update-slice_fusion.37
  36.7 0.8 constant_dynamic-update-slice_fusion.36
  37.6 1.0 constant_dynamic-update-slice_fusion.35
  38.6 0.9 constant_dynamic-update-slice_fusion.20
  39.4 0.9 constant_dynamic-update-slice_fusion.19
  40.3 248.7 %all-reduce.4.cloned.1.call-done = (bf16[32,8192]{1,0:T(8,128)(2,1)}, bf16[32,8192]{1,0:T(8,128)(2,1)}, bf16[32,8192]{1,0:T(8,128)(2,1)}) async-done(((bf16[32,8192]{1,0:T(8,128)(2,1)}, bf16[32,8192]{1,0:T(8,128)(2,1)}, bf16[32,8192]{1,0:T(8,128)(2,1)}), (bf16[32,8192]{1,0:T(8,128)(2,1)}, bf16[32,8192]{1,0:T(8,128)(2,1)}, bf16[32,8192]{1,0:T(8,128)(2,1)})) %all-reduce.4.cloned.1.call-update) | async-done | bytes 1572880 | tf_op jit(solution)/shard_map/psum | solution.py:12
  289.1 1.2 constant_dynamic-update-slice_fusion.2
  290.3 1.1 constant_dynamic-update-slice_fusion.1
  291.4 1.2 constant_dynamic-update-slice_fusion
  292.6 0.7 fusion.18
  293.3 0.9 fusion.19
  294.2 0.7 copy-done.5
  294.9 0.7 fusion.20
  295.6 0.4 copy-done.7
  296.0 0.7 fusion.21
  296.7 0.7 fusion.25
  297.4 2.3 fusion.22
  299.7 2.3 fusion.23
  302.0 2.4 fusion.24
  304.5 0.7 fusion.15
  305.2 0.9 copy-done.21
  306.0 0.7 fusion.13
  306.7 0.2 copy-done.17
  306.9 0.7 fusion.11
  307.6 0.7 copy-done.15
  308.4 0.7 fusion.9
  309.1 0.3 copy-done.9
  309.4 0.7 fusion.7
  310.1 0.7 copy-done.13
  310.7 0.7 fusion.5
  311.5 0.4 copy-done.19
  311.8 0.7 fusion.3
  312.5 0.6 copy-done.11
  313.1 0.7 fusion.1
  313.9 1.0 copy-done.24
  314.9 41.8 %reduce-scatter.2.cloned.1.call-done = f32[96,8,32]{0,2,1:T(8,128)} async-done(((f32[96,64,32]{0,2,1:T(8,128)}), f32[96,8,32]{0,2,1:T(8,128)}) %reduce-scatter.2.cloned.1.call-update) | async-done | bytes 98320 | tf_op jit(solution)/shard_map/reduce_scatter | solution.py:59
  356.6 1.8 copy.6
  (55 shorter events, 1.8 us)
Async XLA Ops:
  6.5 282.5 %all-reduce.4.cloned.1.call-start = ((), (), s32[]{:S(2)}) async-start(), calls=%async_computation.2 | async-start | bytes 3145728 | tf_op jit(solution)/shard_map/psum | solution.py:12
  15.0 341.6 %reduce-scatter.2.cloned.1.call-start = ((), (), s32[]{:S(2)}) async-start(), calls=%async_computation.1 | async-start | bytes 1179648 | tf_op jit(solution)/shard_map/reduce_scatter | solution.py:59
  20.3 1.4 copy-start.20
  20.3 2.0 copy-start.22
  22.3 1.3 copy-start.14
  22.4 3.4 copy-start
  22.4 3.4 copy-start.2
  22.4 5.0 %copy-start.4 = (bf16[8,32,4096]{2,1,0:T(8,128)(2,1)}, bf16[8,32,4096]{2,1,0:T(8,128)(2,1)S(1)}, u32[]{:S(2)}) copy-start(bf16[8,32,4096]{2,1,0:T(8,128)(2,1)S(1)} %get-tuple-element.22) | copy-start | bytes 6291460
  22.4 5.0 %copy-start.6 = (bf16[8,32,4096]{2,1,0:T(8,128)(2,1)}, bf16[8,32,4096]{2,1,0:T(8,128)(2,1)S(1)}, u32[]{:S(2)}) copy-start(bf16[8,32,4096]{2,1,0:T(8,128)(2,1)S(1)} %get-tuple-element.24) | copy-start | bytes 6291460
  22.4 5.0 %copy-start.16 = (bf16[8,32,4096]{2,1,0:T(8,128)(2,1)}, bf16[8,32,4096]{2,1,0:T(8,128)(2,1)S(1)}, u32[]{:S(2)}) copy-start(bf16[8,32,4096]{2,1,0:T(8,128)(2,1)S(1)} %get-tuple-element.26) | copy-start | bytes 6291460
  25.7 4.6 %copy-start.10 = (bf16[8,32,4096]{2,1,0:T(8,128)(2,1)}, bf16[8,32,4096]{2,1,0:T(8,128)(2,1)S(1)}, u32[]{:S(2)}) copy-start(bf16[8,32,4096]{2,1,0:T(8,128)(2,1)S(1)} %get-tuple-element.10) | copy-start | bytes 6291460
  28.7 2.0 copy-start.18
  30.3 1.7 copy-start.12
  32.0 4.7 %copy-start.8 = (bf16[8,32,4096]{2,1,0:T(8,128)(2,1)}, bf16[8,32,4096]{2,1,0:T(8,128)(2,1)S(1)}, u32[]{:S(2)}) copy-start(bf16[8,32,4096]{2,1,0:T(8,128)(2,1)S(1)} %get-tuple-element.104) | copy-start | bytes 6291460
  289.1 3.6 copy-start.1
  291.4 2.0 copy-start.3
  293.3 1.6 copy-start.5
  294.2 1.7 copy-start.7
  302.0 2.5 copy-start.23
  304.4 1.6 copy-start.21
  305.2 1.7 copy-start.17
  306.7 1.6 copy-start.15
  307.6 1.7 copy-start.9
  309.1 1.7 copy-start.13
  310.1 1.7 copy-start.19
  311.5 1.7 copy-start.11
  313.8 1.0 copy-start.24
Sparse Core Ops, SparseCore 0:
  15.1 273.8 all-reduce.3
  315.0 41.5 reduce-scatter.1
where the time goes:
time: 366 us; the launch traced here: 365 us
  waiting for transfers between devices  291 us (80%)
  local copies, waits for them, and re-layouts  37.4 us (10%)
  between operations  16.6 us (5%)
  matrix products  16.3 us (4%)
  other arithmetic  4.4 us (1%)
    psum x1, waiting for transfers between devices, spread(): return lax.psum(kept, axis)  249 us
    reduce_scatter x1, waiting for transfers between devices, body(): reduced = lax.psum_scatter(complete, 'win', scatter_dimension=1, tiled=True)  41.8 us
    unnamed x83, local copies, waits for them, and re-layouts  23.7 us
    dot_general x16, matrix products, correlate(): jnp.einsum('pt,gct->pgc', sources[:, offset:offset + time_block], shifted...  16.3 us
    another operation x7, local copies, waits for them, and re-layouts, correlate(): jnp.stack([padded[:, offset + lag - half_lags + 64:offset + lag - half_la...  9.25 us
  transfers between devices with their start and end apart: 2, of which 2 were waited for; matrix products, arithmetic and copies ran while one was open for 6% of the time, Pallas kernels for 0%

commit v1 on v0

--- a/solution.py
+++ b/solution.py
@@ -9,7 +9,7 @@
 
 def spread(value, axis, source):
     kept = jnp.where(lax.axis_index(axis) == source, value, 0).astype(value.dtype)
-    return lax.psum(kept, axis)
+    return jnp.sum(lax.all_gather(kept, axis), axis=0)
 
 
 def body(traces, owner, window_mask):

time: 366 us -> 511 us (1.40)
  waiting for transfers between devices: 291 us -> 410 us
  other arithmetic: 4.4 us -> 32.1 us
    all_gather x0 -> x3, waiting for transfers between devices: none -> 367 us  [spread(): return jnp.sum(lax.all_gather(kept, axis), axis=0)]
    psum x1 -> x0, waiting for transfers between devices: 249 us -> none  [spread(): return lax.psum(kept, axis)]
    reduce_sum x0 -> x3, other arithmetic: none -> 27.1 us  [spread(): return jnp.sum(lax.all_gather(kept, axis), axis=0)]
    unnamed x83 -> x77, local copies, waits for them, and re-layouts: 23.7 us -> 21 us
  transfers between devices with their start and end apart: 2 -> 4, of which waited for: 2 -> 4; matrix products, arithmetic and copies ran while one was open for 6% -> 8% of each run, Pallas kernels for 0% -> 0%
where the time goes in v1:
time: 511 us
  waiting for transfers between devices  410 us (80%)
  local copies, waits for them, and re-layouts  34.5 us (7%)
  other arithmetic  32.1 us (6%)
  matrix products  18.2 us (4%)
  between operations  16.2 us (3%)
    all_gather x3, waiting for transfers between devices, spread(): return jnp.sum(lax.all_gather(kept, axis), axis=0)  367 us
    reduce_scatter x1, waiting for transfers between devices, body(): reduced = lax.psum_scatter(complete, 'win', scatter_dimension=1, tiled=True)  41.6 us
    reduce_sum x3, other arithmetic, spread(): return jnp.sum(lax.all_gather(kept, axis), axis=0)  27.1 us
    unnamed x77, local copies, waits for them, and re-layouts  21 us
    dot_general x16, matrix products, correlate(): jnp.einsum('pt,gct->pgc', sources[:, offset:offset + time_block], shifted...  18.2 us
  transfers between devices with their start and end apart: 4, of which 4 were waited for; matrix products, arithmetic and copies ran while one was open for 8% of the time, Pallas kernels for 0%

profile of v1, /device:TPU:16, one launch (start us, length us, event | category | flops | bytes accessed | tf_op | source)
XLA Modules:
  0.0 510.6 jit_solution(12498739564118845584)
XLA Ops:
  7.2 1.3 fusion.18
  8.5 1.4 fusion.30
  11.8 2.4 broadcast_select_fusion.2
  14.3 0.7 all-gather.6.cloned.1.call-update
  15.1 0.7 all-gather.8.cloned.1.call-update
  16.0 0.5 constant_dynamic-update-slice_fusion.119
  16.5 0.7 constant_dynamic-update-slice_fusion.127
  17.1 0.6 constant_dynamic-update-slice_fusion.126
  17.8 0.6 constant_dynamic-update-slice_fusion.125
  18.4 0.6 constant_dynamic-update-slice_fusion.124
  19.1 0.6 constant_dynamic-update-slice_fusion.123
  19.7 1.4 constant_dynamic-update-slice_fusion.122
  21.1 0.7 constant_dynamic-update-slice_fusion.121
  21.9 2.1 constant_dynamic-update-slice_fusion.120
  25.3 0.3 constant_dynamic-update-slice_fusion.105
  25.9 0.3 copy-done.9
  26.1 0.5 copy-done.11
  27.1 0.2 copy-done.15
  27.3 1.5 constant_dynamic-update-slice_fusion.104
  28.8 1.7 constant_dynamic-update-slice_fusion.88
  31.0 1.4 constant_dynamic-update-slice_fusion.72
  32.4 1.0 constant_dynamic-update-slice_fusion.51
  33.4 0.9 constant_dynamic-update-slice_fusion.50
  34.2 0.9 constant_dynamic-update-slice_fusion.49
  35.1 1.3 constant_dynamic-update-slice_fusion.48
  36.4 0.8 constant_dynamic-update-slice_fusion.34
  37.3 0.9 constant_dynamic-update-slice_fusion.33
  38.1 1.2 constant_dynamic-update-slice_fusion.32
  39.3 0.9 constant_dynamic-update-slice_fusion.17
  40.2 1.0 constant_dynamic-update-slice_fusion.16
  41.2 110.7 %all-gather.4.cloned.1.call-done = bf16[32,32,8192]{2,1,0:T(8,128)(2,1)} async-done(((bf16[1,32,8192]{2,1,0:T(8,128)(2,1)}), bf16[32,32,8192]{2,1,0:T(8,128)(2,1)}) %all-gather.4.cloned.1.call-update) | async-done | bytes 16777232 | tf_op jit(solution)/shard_map/all_gather | solution.py:12
  151.9 8.9 %reduce_sum.46 = bf16[32,8192]{1,0:T(8,128)(2,1)S(1)} reduce(bf16[32,32,8192]{2,1,0:T(8,128)(2,1)} %all-gather.4.cloned.1.call-done, bf16[]{:T(256)} %constant.21.clone.1), dimensions={0}, to_apply=%region_1.2 | reduce | flops 8126464 | bytes 17301506 | tf_op jit(solution)/shard_map/reduce_sum | solution.py:12
  160.8 127.8 %all-gather.6.cloned.1.call-done = bf16[32,32,8192]{2,1,0:T(8,128)(2,1)} async-done(((bf16[1,32,8192]{2,1,0:T(8,128)(2,1)}), bf16[32,32,8192]{2,1,0:T(8,128)(2,1)}) %all-gather.6.cloned.1.call-update) | async-done | bytes 16777232 | tf_op jit(solution)/shard_map/all_gather | solution.py:12
  288.6 8.7 %reduce_sum.47 = bf16[32,8192]{1,0:T(8,128)(2,1)S(1)} reduce(bf16[32,32,8192]{2,1,0:T(8,128)(2,1)} %all-gather.6.cloned.1.call-done, bf16[]{:T(256)} %constant.21.clone.1), dimensions={0}, to_apply=%region_2.3 | reduce | flops 8126464 | bytes 17301506 | tf_op jit(solution)/shard_map/reduce_sum | solution.py:12
  297.3 128.0 %all-gather.8.cloned.1.call-done = bf16[32,32,8192]{2,1,0:T(8,128)(2,1)} async-done(((bf16[1,32,8192]{2,1,0:T(8,128)(2,1)}), bf16[32,32,8192]{2,1,0:T(8,128)(2,1)}) %all-gather.8.cloned.1.call-update) | async-done | bytes 16777232 | tf_op jit(solution)/shard_map/all_gather | solution.py:12
  425.3 9.5 %reduce_sum.48 = bf16[32,8192]{1,0:T(8,128)(2,1)} reduce(bf16[32,32,8192]{2,1,0:T(8,128)(2,1)} %all-gather.8.cloned.1.call-done, bf16[]{:T(256)} %constant.21.clone.1), dimensions={0}, to_apply=%region_3.4 | reduce | flops 8126464 | bytes 17301506 | tf_op jit(solution)/shard_map/reduce_sum | solution.py:12
  434.8 1.1 pad_maximum_fusion
  436.0 0.7 fusion.22
  436.7 0.8 copy-done.2
  437.5 0.7 fusion.23
  438.4 0.7 fusion.24
  439.2 0.7 copy-done.6
  439.9 0.7 fusion.25
  440.6 2.3 fusion.26
  442.9 2.3 fusion.27
  445.3 2.3 fusion.28
  447.6 2.5 fusion.29
  450.1 0.7 fusion.17
  450.8 0.8 copy-done.12
  451.7 0.7 fusion.15
  452.6 0.7 fusion.13
  453.3 0.7 copy-done.8
  454.0 0.7 fusion.11
  454.8 0.3 copy-done.22
  455.0 0.7 fusion.9
  455.8 0.6 copy-done.14
  456.4 0.7 fusion.7
  457.2 0.4 copy-done.18
  457.5 0.7 fusion.5
  458.3 0.6 copy-done.16
  458.9 0.7 fusion.3
  459.6 1.0 copy-done.23
  460.6 41.6 %reduce-scatter.2.cloned.1.call-done = f32[96,8,32]{0,2,1:T(8,128)} async-done(((f32[96,64,32]{0,2,1:T(8,128)}), f32[96,8,32]{0,2,1:T(8,128)}) %reduce-scatter.2.cloned.1.call-update) | async-done | bytes 98320 | tf_op jit(solution)/shard_map/reduce_scatter | solution.py:59
  502.2 1.8 copy.7
  (58 shorter events, 3.0 us)
Async XLA Ops:
  6.5 145.4 %all-gather.4.cloned.1.call-start = ((), (), s32[]{:S(2)}) async-start(), calls=%async_computation.1 | async-start | bytes 17301504 | tf_op jit(solution)/shard_map/all_gather | solution.py:12
  7.2 8.6 %copy-start = (bf16[1,32,8192]{2,1,0:T(8,128)(2,1)S(1)}, bf16[1,32,8192]{2,1,0:T(8,128)(2,1)}, u32[]{:S(2)}) copy-start(bf16[1,32,8192]{2,1,0:T(8,128)(2,1)} %param.3) | copy-start | bytes 1572868
  14.3 274.3 %all-gather.6.cloned.1.call-start = ((), (), s32[]{:S(2)}) async-start(), calls=%async_computation.2 | async-start | bytes 17301504 | tf_op jit(solution)/shard_map/all_gather | solution.py:12
  15.0 410.3 %all-gather.8.cloned.1.call-start = ((), (), s32[]{:S(2)}) async-start(), calls=%async_computation.3 | async-start | bytes 17301504 | tf_op jit(solution)/shard_map/all_gather | solution.py:12
  15.7 486.5 %reduce-scatter.2.cloned.1.call-start = ((), (), s32[]{:S(2)}) async-start(), calls=%async_computation.4 | async-start | bytes 1179648 | tf_op jit(solution)/shard_map/reduce_scatter | solution.py:59
  21.9 2.5 copy-start.1
  21.9 2.5 copy-start.3
  21.9 3.9 copy-start.5
  21.9 3.9 copy-start.7
  21.9 4.2 copy-start.9
  21.9 4.7 copy-start.11
  24.0 3.3 copy-start.15
  25.5 3.3 copy-start.19
  28.8 2.2 copy-start.17
  30.5 1.8 copy-start.13
  32.4 4.9 copy-start.21
  436.0 1.6 copy-start.2
  436.7 1.7 copy-start.4
  438.3 1.6 copy-start.6
  447.6 2.5 copy-start.20
  450.1 1.6 copy-start.12
  450.8 1.7 copy-start.10
  452.4 1.6 copy-start.8
  453.3 1.8 copy-start.22
  454.8 1.7 copy-start.14
  455.8 1.8 copy-start.18
  457.2 1.7 copy-start.16
  459.6 1.0 copy-start.23
Sparse Core Ops, SparseCore 0:
  14.4 137.4 all-gather.3
  154.7 133.8 all-gather.5
  291.4 133.8 all-gather.7
  460.7 41.4 reduce-scatter.1
